TPU v7x, 32 devices: a whole 2x2x4 slice. The times are simulated.
32 devices in a mesh: ctx: 8 (over z, y), roll: 4 (over x, core).
Axes of the slice: x: 2, y: 2, z: 4, core: 2. Of those that a mesh axis runs over, the one named last changes fastest.
Arguments:
- block_order: int32 [8], replicated, may hold values from 0 to 7, as said below
- segment_ids: int32 [1024], replicated, may hold values from 0 to 3, as said below
- layer_input: bfloat16 [8192, 1024], P(None, 'ctx'), may hold values from -6 to 6
- query_states: bfloat16 [1024, 768], P('ctx')
- key_states: bfloat16 [1024, 128], P('ctx')
- value_states: bfloat16 [1024, 128], P('ctx'), may hold values from -6 to 6
- out_grad: bfloat16 [1024, 768], P('ctx'), may hold values from -24 to 24
- master_weight: float32 [8192, 128], P(('ctx', 'roll')), may hold values from -0.0625 to 0.0625
- first_moment: float32 [8192, 128], P(('ctx', 'roll')), may hold values from -60 to 60
- second_moment: float32 [8192, 128], P(('ctx', 'roll')), may hold values from 30 to 3000
Outputs:
- query_grad: bfloat16 [1024, 768], P('ctx')
- key_value_grad: bfloat16 [1024, 256], P('ctx')
- updated_master: float32 [8192, 128], P(('ctx', 'roll'))
- updated_first: float32 [8192, 128], P(('ctx', 'roll'))
- updated_second: float32 [8192, 128], P(('ctx', 'roll'))
- rollout_weight: bfloat16 [8192, 128], P('ctx')
Inputs may be any that keep to these rules, and one draw needn't show every extreme that they name: A permutation: index c of ctx holds the tokens at positions block_order[c] * 128 to block_order[c] * 128 + 127, in order; every block is held once. `segment_ids`: ids never fall along sequence positions; there are exactly 4 rollouts; no rollout begins at offset 128 // 2 of a block.
All inputs are finite; a program needn't handle non-finite values.
Results may differ from a plain program's by a relative error of at most 0.028.
Values may be sent and summed in bfloat16 or wider, within the bound.
No kernel may reach another device: no remote copies, remote signals or barrier semaphores. Data moves between devices by JAX's collectives and lax.ppermute only.
A program may use at most 64 MiB of HBM per device.

v0:
```python
import math

import jax
import jax.numpy as jnp
from jax import lax
from jax.sharding import PartitionSpec as P

NEG_FILL = -1e30
BETA_ONE = 0.9
BETA_TWO = 0.95
ADAM_EPS = 1e-08
DECAY_RATE = 0.1
LEARN_RATE = 1e-06
CORRECT_ONE = 0.9999734386011124
CORRECT_TWO = 0.994079470779666


def joined(part, axis, combine):
    gathered = jax.tree.map(lambda a: lax.all_gather(a, axis), part)

    def take(source):
        return jax.tree.map(lambda a: lax.dynamic_index_in_dim(a, source, 0, False), gathered)

    return lax.fori_loop(
        1, lax.axis_size(axis), lambda source, state: combine(state, take(source)), take(0)
    )


def contract_last(left_side, right_side):
    return lax.dot_general(
        left_side, right_side, (((1,), (1,)), ((), ())), preferred_element_type=jnp.float32
    )


def contract_first(left_side, right_side):
    return lax.dot_general(
        left_side, right_side, (((0,), (0,)), ((), ())), preferred_element_type=jnp.float32
    )


def visible_rows(q_pos, q_seg, key_pos, key_seg, head_group):
    visible = (key_pos[None, :] <= q_pos[:, None]) & (key_seg[None, :] == q_seg[:, None])
    return jnp.repeat(visible, head_group, axis=0)


def key_block_data(key_all, value_all, key_pos, key_seg):
    return (key_all, value_all, key_pos, key_seg)


def softmax_stats(
    q_rows, do_rows, key_all, value_all, key_pos, key_seg, q_pos, q_seg, head_group, score_scale
):
    block_width = math.gcd(key_all.shape[0], 512)
    row_total = q_rows.shape[0]

    def softmax_advance(step_index, carry):
        row_top, row_sum, weighted = carry
        key_block, value_block, pos_block, seg_block = key_block_data(
            key_all, value_all, key_pos, key_seg
        )
        visible = visible_rows(q_pos, q_seg, pos_block, seg_block, head_group)
        scores = jnp.where(visible, contract_last(q_rows, key_block) * score_scale, NEG_FILL)
        new_top = jnp.maximum(row_top, jnp.max(scores, axis=1))
        expo = jnp.where(visible, jnp.exp(scores - new_top[:, None]), 0.0)
        dprob = contract_last(do_rows, value_block)
        factor = jnp.exp(row_top - new_top)
        return (
            new_top,
            row_sum * factor + jnp.sum(expo, axis=1),
            weighted * factor + jnp.sum(expo * dprob, axis=1),
        )

    start_state = (
        jnp.full((row_total,), NEG_FILL, jnp.float32),
        jnp.zeros((row_total,), jnp.float32),
        jnp.zeros((row_total,), jnp.float32),
    )
    return lax.fori_loop(0, key_all.shape[0] // block_width, softmax_advance, start_state)


def gradient_pass(
    q_rows,
    do_rows,
    key_all,
    value_all,
    key_pos,
    key_seg,
    q_pos,
    q_seg,
    log_total,
    delta,
    head_group,
    score_scale,
):
    key_count, head_dim = key_all.shape
    block_width = math.gcd(key_count, 512)

    def gradient_advance(step_index, carry):
        query_acc, term = carry
        key_block, value_block, pos_block, seg_block = key_block_data(
            key_all, value_all, key_pos, key_seg
        )
        visible = visible_rows(q_pos, q_seg, pos_block, seg_block, head_group)
        scores = jnp.where(visible, contract_last(q_rows, key_block) * score_scale, NEG_FILL)
        weights = jnp.where(visible, jnp.exp(scores - log_total[:, None]), 0.0)
        dprob = contract_last(do_rows, value_block)
        dscore = weights * (dprob - delta[:, None])
        weights_half = weights.astype(jnp.bfloat16)
        dscore_half = dscore.astype(jnp.bfloat16)
        query_acc = query_acc + jnp.dot(dscore_half, key_block, preferred_element_type=jnp.float32)
        key_part = contract_first(dscore_half, q_rows) * score_scale
        value_part = contract_first(weights_half, do_rows)
        term = jnp.concatenate([key_part, value_part], axis=1)
        return (query_acc, term)

    start_state = (
        jnp.zeros((q_rows.shape[0], head_dim), jnp.float32),
        jnp.zeros((key_count, 2 * head_dim), jnp.float32),
    )
    return lax.fori_loop(0, key_count // block_width, gradient_advance, start_state)


def combine_stats(first_side, second_side):
    row_top = jnp.maximum(first_side[0], second_side[0])
    first_scale = jnp.exp(first_side[0] - row_top)
    second_scale = jnp.exp(second_side[0] - row_top)
    return (
        row_top,
        first_side[1] * first_scale + second_side[1] * second_scale,
        first_side[2] * first_scale + second_side[2] * second_scale,
    )


def body(
    block_order,
    segment_ids,
    layer_input,
    query_states,
    key_states,
    value_states,
    out_grad,
    master_weight,
    first_moment,
    second_moment,
):
    row_count, head_dim = key_states.shape
    head_group = query_states.shape[1] // head_dim
    ctx_count = lax.axis_size("ctx")
    roll_count = lax.axis_size("roll")
    ctx_rank = lax.axis_index("ctx")
    roll_rank = lax.axis_index("roll")
    score_scale = head_dim ** (-0.5)
    offsets = jnp.arange(row_count, dtype=jnp.int32)
    pos_table = block_order[:, None] * row_count + offsets[None, :]
    seg_table = segment_ids.reshape(ctx_count, row_count)
    q_pos = lax.dynamic_index_in_dim(pos_table, ctx_rank, 0, keepdims=False)
    q_seg = lax.dynamic_index_in_dim(seg_table, ctx_rank, 0, keepdims=False)
    q_rows = query_states.reshape(row_count * head_group, head_dim)
    do_rows = out_grad.reshape(row_count * head_group, head_dim)
    share_rows = row_count // roll_count
    first_row = roll_rank * share_rows
    key_all, value_all = (
        lax.all_gather(
            lax.dynamic_slice_in_dim(key_states, first_row, share_rows, 0),
            "ctx",
            axis=0,
            tiled=True,
        ),
        lax.all_gather(
            lax.dynamic_slice_in_dim(value_states, first_row, share_rows, 0),
            "ctx",
            axis=0,
            tiled=True,
        ),
    )
    key_pos = lax.dynamic_slice_in_dim(pos_table, first_row, share_rows, 1).reshape(-1)
    key_seg = lax.dynamic_slice_in_dim(seg_table, first_row, share_rows, 1).reshape(-1)
    part_top, part_sum, part_weighted = softmax_stats(
        q_rows, do_rows, key_all, value_all, key_pos, key_seg, q_pos, q_seg, head_group, score_scale
    )
    row_top, row_sum, weighted = joined((part_top, part_sum, part_weighted), "roll", combine_stats)
    log_total = row_top + jnp.log(row_sum)
    delta = weighted / row_sum
    query_acc, term = gradient_pass(
        q_rows,
        do_rows,
        key_all,
        value_all,
        key_pos,
        key_seg,
        q_pos,
        q_seg,
        log_total,
        delta,
        head_group,
        score_scale,
    )
    key_value = lax.psum_scatter(term.astype(jnp.bfloat16), "ctx", scatter_dimension=0, tiled=True)
    query_acc = lax.psum(query_acc.astype(jnp.bfloat16), "roll").astype(jnp.float32)
    key_value = lax.all_gather(key_value, "roll", axis=0, tiled=True)
    query_grad = (
        (query_acc * score_scale).astype(jnp.bfloat16).reshape(row_count, head_group * head_dim)
    )
    key_grad = key_value[:, :head_dim]
    owner_rows = master_weight.shape[0]
    picked = lax.dynamic_index_in_dim(
        layer_input.reshape(ctx_count, roll_count, owner_rows, row_count),
        roll_rank,
        1,
        keepdims=False,
    )
    feature_cols = lax.all_to_all(picked, "ctx", split_axis=0, concat_axis=2, tiled=True)
    token_grads = lax.all_gather(key_grad, "ctx", axis=0, tiled=True)
    block_terms = jnp.einsum(
        "scr,crh->csh",
        feature_cols.reshape(owner_rows, ctx_count, row_count),
        token_grads.reshape(ctx_count, row_count, head_dim),
        preferred_element_type=jnp.float32,
    )
    rounded = lax.optimization_barrier(block_terms.astype(jnp.bfloat16))
    weight_grad = jnp.sum(rounded.astype(jnp.float32), axis=0)
    updated_first = BETA_ONE * first_moment + (1.0 - BETA_ONE) * weight_grad
    updated_second = BETA_TWO * second_moment + (1.0 - BETA_TWO) * weight_grad * weight_grad
    update = (
        updated_first / CORRECT_ONE / (jnp.sqrt(updated_second / CORRECT_TWO) + ADAM_EPS)
        + DECAY_RATE * master_weight
    )
    updated_master = master_weight - LEARN_RATE * update
    rollout_weight = lax.all_gather(updated_master.astype(jnp.bfloat16), "roll", axis=0, tiled=True)
    return (query_grad, key_value, updated_master, updated_first, updated_second, rollout_weight)


def solution(mesh):
    placed = (
        P(),
        P(),
        P(None, "ctx"),
        P("ctx", None),
        P("ctx", None),
        P("ctx", None),
        P("ctx", None),
        P(("ctx", "roll"), None),
        P(("ctx", "roll"), None),
        P(("ctx", "roll"), None),
    )
    return jax.shard_map(
        body,
        mesh=mesh,
        in_specs=placed,
        out_specs=(
            P("ctx", None),
            P("ctx", None),
            P(("ctx", "roll"), None),
            P(("ctx", "roll"), None),
            P(("ctx", "roll"), None),
            P("ctx", None),
        ),
        check_vma=False,
    )
```

profile of v0, /device:TPU:0, one launch (start us, length us, event | category | flops | bytes accessed | tf_op | source)
XLA Modules:
  0.0 233.1 jit_solution(4776817111564583894)
XLA Ops:
  8.0 1.5 copy-done
  9.6 0.9 dynamic-slice_bitcast_fusion
  10.5 7.3 %all-to-all-start = ((bf16[8,256,128]{2,1,0:T(8,128)(2,1)}), bf16[8,256,128]{2,1,0:T(8,128)(2,1)}, u32[]{:S(2)}, u32[]{:S(2)}) async-start(bf16[8,256,128]{2,1,0:T(8,128)(2,1)} %dynamic-slice_bitcast_fusion), calls=%async_computation | async-start | bytes 1048576 | tf_op jit(solution)/shard_map/all_to_all | solution.py:212
  19.6 35.5 %all_gather.27 = bf16[256,128]{1,0:T(8,128)(2,1)S(1)} all-gather(bf16[32,128]{1,0:T(8,128)(2,1)S(1)} %constant_dynamic-slice_fusion.1), channel_id=1, replica_groups=mesh['ctx'=8,'roll'=4] {'ctx'}, dimensions={0}, use_global_device_ids=true | all-gather | bytes 73728 | tf_op jit(solution)/shard_map/all_gather | solution.py:163
  56.3 32.5 %all_gather.30 = bf16[256,128]{1,0:T(8,128)(2,1)} all-gather(bf16[32,128]{1,0:T(8,128)(2,1)S(1)} %constant_dynamic-slice_fusion), channel_id=1, replica_groups=mesh['ctx'=8,'roll'=4] {'ctx'}, dimensions={0}, use_global_device_ids=true | all-gather | bytes 73728 | tf_op jit(solution)/shard_map/all_gather | solution.py:169
  88.8 1.1 reshape.96
  89.9 2.1 multiply_reduce_fusion
  92.0 5.2 %all-gather.3 = f32[4,1,768]{2,1,0:T(1,128)S(1)} all-gather(f32[1,1,768]{2,1,0:T(1,128)S(1)} %reshape.115), channel_id=1, replica_groups=mesh['ctx'=8,'roll'=4] {'roll'}, dimensions={0}, use_global_device_ids=true | all-gather | bytes 15360 | tf_op jit(solution)/shard_map/all_gather | solution.py:19
  97.8 5.2 %all-gather.2 = f32[4,1,768]{2,1,0:T(1,128)S(1)} all-gather(f32[1,1,768]{2,1,0:T(1,128)S(1)} %reshape.113), channel_id=1, replica_groups=mesh['ctx'=8,'roll'=4] {'roll'}, dimensions={0}, use_global_device_ids=true | all-gather | bytes 15360 | tf_op jit(solution)/shard_map/all_gather | solution.py:19
  103.6 5.2 %all-gather.1 = f32[4,1,768]{2,1,0:T(1,128)S(1)} all-gather(f32[1,1,768]{2,1,0:T(1,128)S(1)} %reshape.111), channel_id=2, replica_groups=mesh['ctx'=8,'roll'=4] {'roll'}, dimensions={0}, use_global_device_ids=true | all-gather | bytes 15360 | tf_op jit(solution)/shard_map/all_gather | solution.py:19
  109.5 4.7 %while.12 = (s32[]{:T(128)}, f32[768]{0:T(1024)S(1)}, f32[768]{0:T(1024)S(1)}, f32[768]{0:T(1024)S(1)}, f32[4,768]{1,0:T(4,128)}, /*index=5*/f32[4,768]{1,0:T(4,...) while((s32[]{:T(128)}, f32[768]{0:T(1024)S(1)}, f32[768]{0:T(1024)S(1)}, f32[768]{0:T(1024)S(1)}, ...), condition=%wide.region_4.5_spmd, body=%wide.region_3.4_spmd.sunk | while | flops 8453 | bytes 61591 | solution.py:24
  114.1 1.4 multiply_convert_fusion
  115.5 1.0 convolution_convert_fusion.1
  116.6 1.2 fusion.2
  117.8 1.3 convolution_convert_fusion.2
  119.9 26.1 %all-reduce.2.cloned.1.call-done = bf16[768,128]{1,0:T(8,128)(2,1)} async-done(((bf16[768,128]{1,0:T(8,128)(2,1)}), bf16[768,128]{1,0:T(8,128)(2,1)}) %all-reduce.2.cloned.1.call-update) | async-done | bytes 196624 | tf_op jit(solution)/shard_map/psum | solution.py:199
  145.9 1.0 multiply_convert_fusion.1
  146.9 0.9 reshape.97
  147.8 32.3 %reduce-scatter.4.cloned.1.call-done = bf16[32,256]{1,0:T(8,128)(2,1)} async-done(((bf16[256,256]{1,0:T(8,128)(2,1)}), bf16[32,256]{1,0:T(8,128)(2,1)}) %reduce-scatter.4.cloned.1.call-update) | async-done | bytes 16400 | tf_op jit(solution)/shard_map/reduce_scatter | solution.py:198
  180.1 5.4 %all_gather.32 = bf16[128,256]{1,0:T(8,128)(2,1)S(1)} all-gather(bf16[32,256]{1,0:T(8,128)(2,1)} %reduce-scatter.4.cloned.1.call-done), channel_id=1, replica_groups=mesh['ctx'=8,'roll'=4] {'roll'}, dimensions={0}, use_global_device_ids=true | all-gather | bytes 81920 | tf_op jit(solution)/shard_map/all_gather | solution.py:200
  185.5 30.7 %all_gather.33 = bf16[1024,128]{1,0:T(8,128)(2,1)S(1)} all-gather(bf16[128,128]{1,0:T(8,128)(2,1)S(1)} %slice.14), channel_id=1, replica_groups=mesh['ctx'=8,'roll'=4] {'ctx'}, dimensions={0}, use_global_device_ids=true | all-gather | bytes 294912 | tf_op jit(solution)/shard_map/all_gather | solution.py:213
  216.3 1.3 convolution_convert_fusion
  217.7 0.8 fusion.15
  218.5 5.8 %all_gather.34 = bf16[1024,128]{1,0:T(8,128)(2,1)S(1)} all-gather(bf16[256,128]{1,0:T(8,128)(2,1)S(1)} %get-tuple-element.291), channel_id=1, replica_groups=mesh['ctx'=8,'roll'=4] {'roll'}, dimensions={0}, use_global_device_ids=true | all-gather | bytes 327680 | tf_op jit(solution)/shard_map/all_gather | solution.py:229
  (69 shorter events, 11.6 us)
Async XLA Ops:
  8.0 1.6 copy-start
  8.0 9.8 %copy-start.8 = (s32[8]{0:T(128)S(1)}, s32[8]{0:T(128)}, u32[]{:S(2)}) copy-start(s32[8]{0:T(128)} %param.12) | copy-start | bytes 100
  8.0 9.9 %copy-start.7 = (s32[1024]{0:T(1024)S(1)}, s32[1024]{0:T(1024)}, u32[]{:S(2)}) copy-start(s32[1024]{0:T(1024)} %param.13) | copy-start | bytes 12292
  8.0 47.0 %copy-start.3 = (bf16[128,768]{1,0:T(8,128)(2,1)S(1)}, bf16[128,768]{1,0:T(8,128)(2,1)}, u32[]{:S(2)}) copy-start(bf16[128,768]{1,0:T(8,128)(2,1)} %param.15) | copy-start | bytes 589828
  10.5 205.8 %all-to-all-start = ((bf16[8,256,128]{2,1,0:T(8,128)(2,1)}), bf16[8,256,128]{2,1,0:T(8,128)(2,1)}, u32[]{:S(2)}, u32[]{:S(2)}) async-start(bf16[8,256,128]{2,1,0:T(8,128)(2,1)} %dynamic-slice_bitcast_fusion), calls=%async_computation | async-start | bytes 1048576 | tf_op jit(solution)/shard_map/all_to_all | solution.py:212
  17.8 128.2 %all-reduce.2.cloned.1.call-start = ((), (), s32[]{:S(2)}) async-start(), calls=%async_computation.2 | async-start | bytes 393216 | tf_op jit(solution)/shard_map/psum | solution.py:199
  55.3 54.2 %copy-start.1 = (bf16[768,128]{1,0:T(8,128)(2,1)}, bf16[768,128]{1,0:T(8,128)(2,1)S(1)}, u32[]{:S(2)}) copy-start(bf16[768,128]{1,0:T(8,128)(2,1)S(1)} %reshape.95) | copy-start | bytes 589828
  89.9 24.2 %copy-start.2 = (bf16[768,128]{1,0:T(8,128)(2,1)}, bf16[768,128]{1,0:T(8,128)(2,1)S(1)}, u32[]{:S(2)}) copy-start(bf16[768,128]{1,0:T(8,128)(2,1)S(1)} %reshape.96) | copy-start | bytes 589828
  116.5 63.6 %reduce-scatter.4.cloned.1.call-start = ((), (), s32[]{:S(2)}) async-start(), calls=%async_computation.3 | async-start | bytes 147456 | tf_op jit(solution)/shard_map/reduce_scatter | solution.py:198
  119.0 98.6 %copy-start.4 = (f32[256,128]{1,0:T(8,128)S(1)}, f32[256,128]{1,0:T(8,128)}, u32[]{:S(2)}) copy-start(f32[256,128]{1,0:T(8,128)} %param.19) | copy-start | bytes 393220
  119.1 98.6 %copy-start.5 = (f32[256,128]{1,0:T(8,128)S(1)}, f32[256,128]{1,0:T(8,128)}, u32[]{:S(2)}) copy-start(f32[256,128]{1,0:T(8,128)} %param.20) | copy-start | bytes 393220
  119.1 98.6 %copy-start.6 = (f32[256,128]{1,0:T(8,128)S(1)}, f32[256,128]{1,0:T(8,128)}, u32[]{:S(2)}) copy-start(f32[256,128]{1,0:T(8,128)} %param.21) | copy-start | bytes 393220
Sparse Core Ops, SparseCore 0:
  116.6 29.2 all-reduce.1
Sparse Core Ops, SparseCore 1:
  120.9 59.2 reduce-scatter.3
where the time goes:
time: 234 us; the launch traced here: 233 us
  blocking collectives  126 us (54%)
  waiting for transfers between devices  58.4 us (25%)
  between operations  15.7 us (7%)
  local copies, waits for them, and re-layouts  15.2 us (6%)
  starting transfers between devices  7.39 us (3%)
  matrix products  7.15 us (3%)
  other arithmetic  3.48 us (1%)
    all_gather x1, blocking collectives, body(): lax.all_gather(lax.dynamic_slice_in_dim(key_states, first_row, share_rows...  35.5 us
    all_gather x1, blocking collectives, body(): lax.all_gather(lax.dynamic_slice_in_dim(value_states, first_row, share_ro...  32.5 us
    reduce_scatter x1, waiting for transfers between devices, body(): lax.psum_scatter(term.astype(jnp.bfloat16), 'ctx', scatter_dimension=0, t...  32.3 us
    all_gather x1, blocking collectives, body(): token_grads = lax.all_gather(key_grad, 'ctx', axis=0, tiled=True)  30.7 us
    psum x1, waiting for transfers between devices, body(): lax.psum(query_acc.astype(jnp.bfloat16), 'roll').astype(jnp.float32)  26.1 us
    all_gather x3, blocking collectives, joined(): gathered = jax.tree.map(lambda a: lax.all_gather(a, axis), part)  15.6 us
    all_to_all x1, starting transfers between devices, body(): lax.all_to_all(picked, 'ctx', split_axis=0, concat_axis=2, tiled=True)  7.31 us
    all_gather x1, blocking collectives, body(): lax.all_gather(updated_master.astype(jnp.bfloat16), 'roll', axis=0, tiled...  5.76 us
  transfers between devices with their start and end apart: 3, of which 2 were waited for; matrix products, arithmetic and copies ran while one was open for 9% of the time, Pallas kernels for 0%

commit v1 on v0

v1 whole, which is shorter than its diff:
```python
import jax
import jax.numpy as jnp
from jax import lax
from jax.sharding import PartitionSpec as P

NEG_FILL = -1e30
BETA_ONE = 0.9
BETA_TWO = 0.95
ADAM_EPS = 1e-08
DECAY_RATE = 0.1
LEARN_RATE = 1e-06
CORRECT_ONE = 0.9999734386011124
CORRECT_TWO = 0.994079470779666


def shifted(value, axis, count, shift):
    return lax.ppermute(value, axis, [(i, (i + shift) % count) for i in range(count)])


def body(
    block_order,
    segment_ids,
    layer_input,
    query_states,
    key_states,
    value_states,
    out_grad,
    master_weight,
    first_moment,
    second_moment,
):
    row_count, head_dim = key_states.shape
    head_group = query_states.shape[1] // head_dim
    ctx_count = lax.axis_size("ctx")
    roll_count = lax.axis_size("roll")
    ctx_rank = lax.axis_index("ctx")
    roll_rank = lax.axis_index("roll")
    score_scale = head_dim ** (-0.5)

    offsets = jnp.arange(row_count, dtype=jnp.int32)
    pos_table = block_order[:, None] * row_count + offsets[None, :]
    seg_table = segment_ids.reshape(ctx_count, row_count)
    q_pos = lax.dynamic_index_in_dim(pos_table, ctx_rank, 0, keepdims=False)
    q_seg = lax.dynamic_index_in_dim(seg_table, ctx_rank, 0, keepdims=False)

    own_kv = jnp.concatenate([key_states, value_states], axis=1)
    kv_blocks = [own_kv] + [
        shifted(own_kv, "ctx", ctx_count, s) for s in range(1, ctx_count)
    ]
    kv_all = jnp.concatenate(kv_blocks, axis=0)
    key_all = kv_all[:, :head_dim]
    value_all = kv_all[:, head_dim:]
    sources = (ctx_rank - jnp.arange(ctx_count, dtype=jnp.int32)) % ctx_count
    key_pos = jnp.take(pos_table, sources, axis=0).reshape(-1)
    key_seg = jnp.take(seg_table, sources, axis=0).reshape(-1)

    q_rows = query_states.reshape(row_count * head_group, head_dim)
    do_rows = out_grad.reshape(row_count * head_group, head_dim)
    visible = (key_pos[None, :] <= q_pos[:, None]) & (key_seg[None, :] == q_seg[:, None])
    visible = jnp.repeat(visible, head_group, axis=0)
    scores = jnp.dot(q_rows, key_all.T, preferred_element_type=jnp.float32) * score_scale
    scores = jnp.where(visible, scores, NEG_FILL)
    row_top = jnp.max(scores, axis=1, keepdims=True)
    expo = jnp.where(visible, jnp.exp(scores - row_top), 0.0)
    log_total = row_top + jnp.log(jnp.sum(expo, axis=1, keepdims=True))
    weights = jnp.where(visible, jnp.exp(scores - log_total), 0.0)
    dprob = jnp.dot(do_rows, value_all.T, preferred_element_type=jnp.float32)
    delta = jnp.sum(weights * dprob, axis=1, keepdims=True)
    dscore = weights * (dprob - delta)
    weights_half = weights.astype(jnp.bfloat16)
    dscore_half = dscore.astype(jnp.bfloat16)
    query_part = jnp.dot(dscore_half, key_all, preferred_element_type=jnp.float32) * score_scale
    query_grad = query_part.astype(jnp.bfloat16).reshape(row_count, head_group * head_dim)
    key_part = jnp.dot(dscore_half.T, q_rows, preferred_element_type=jnp.float32) * score_scale
    value_part = jnp.dot(weights_half.T, do_rows, preferred_element_type=jnp.float32)
    part_half = jnp.concatenate([key_part, value_part], axis=1).astype(jnp.bfloat16)
    part_blocks = part_half.reshape(ctx_count, row_count, 2 * head_dim)

    kv_sum = part_blocks[0].astype(jnp.float32)
    for s in range(1, ctx_count):
        kv_sum = kv_sum + shifted(part_blocks[s], "ctx", ctx_count, -s).astype(jnp.float32)
    key_value = kv_sum.astype(jnp.bfloat16)
    key_grad = key_value[:, :head_dim]

    owner_rows = master_weight.shape[0]
    picked = lax.dynamic_index_in_dim(
        layer_input.reshape(ctx_count, roll_count, owner_rows, row_count),
        roll_rank,
        1,
        keepdims=False,
    )
    products = jnp.einsum(
        "csr,rh->csh", picked, key_grad, preferred_element_type=jnp.float32
    ).astype(jnp.bfloat16)
    weight_grad = lax.dynamic_index_in_dim(products, ctx_rank, 0, keepdims=False).astype(
        jnp.float32
    )
    for s in range(1, ctx_count):
        outgoing = lax.dynamic_index_in_dim(
            products, (ctx_rank + s) % ctx_count, 0, keepdims=False
        )
        weight_grad = weight_grad + shifted(outgoing, "ctx", ctx_count, s).astype(jnp.float32)

    updated_first = BETA_ONE * first_moment + (1.0 - BETA_ONE) * weight_grad
    updated_second = BETA_TWO * second_moment + (1.0 - BETA_TWO) * weight_grad * weight_grad
    update = (
        updated_first / CORRECT_ONE / (jnp.sqrt(updated_second / CORRECT_TWO) + ADAM_EPS)
        + DECAY_RATE * master_weight
    )
    updated_master = master_weight - LEARN_RATE * update
    rollout_weight = lax.all_gather(updated_master.astype(jnp.bfloat16), "roll", axis=0, tiled=True)
    return (query_grad, key_value, updated_master, updated_first, updated_second, rollout_weight)


def solution(mesh):
    placed = (
        P(),
        P(),
        P(None, "ctx"),
        P("ctx", None),
        P("ctx", None),
        P("ctx", None),
        P("ctx", None),
        P(("ctx", "roll"), None),
        P(("ctx", "roll"), None),
        P(("ctx", "roll"), None),
    )
    return jax.shard_map(
        body,
        mesh=mesh,
        in_specs=placed,
        out_specs=(
            P("ctx", None),
            P("ctx", None),
            P(("ctx", "roll"), None),
            P(("ctx", "roll"), None),
            P(("ctx", "roll"), None),
            P("ctx", None),
        ),
        check_vma=False,
    )
```

time: 234 us -> 85.4 us (0.36)
  blocking collectives: 126 us -> 5.76 us
  waiting for transfers between devices: 58.4 us -> 8.04 us
  starting transfers between devices: 7.39 us -> 33.1 us
  between operations: 15.7 us -> 0.82 us
  local copies, waits for them, and re-layouts: 15.2 us -> 23.6 us
    all_gather x7 -> x0, blocking collectives: 120 us -> none  [the longest x1 35.5 us: body(): lax.all_gather(lax.dynamic_slice_in_dim(key_states, first_row, share_rows...]
    ppermute x0 -> x21, starting transfers between devices: none -> 33.1 us  [shifted(): lax.ppermute(value, axis, [(i, (i + shift) % count) for i in range(count)])]
    reduce_scatter x1 -> x0, waiting for transfers between devices: 32.3 us -> none  [body(): lax.psum_scatter(term.astype(jnp.bfloat16), 'ctx', scatter_dimension=0, t...]
    psum x1 -> x0, waiting for transfers between devices: 26.1 us -> none  [body(): lax.psum(query_acc.astype(jnp.bfloat16), 'roll').astype(jnp.float32)]
    ppermute x0 -> x21, waiting for transfers between devices: none -> 8.04 us  [shifted(): lax.ppermute(value, axis, [(i, (i + shift) % count) for i in range(count)])]
    all_to_all x1 -> x0, starting transfers between devices: 7.31 us -> none  [body(): lax.all_to_all(picked, 'ctx', split_axis=0, concat_axis=2, tiled=True)]
    unnamed x27 -> x19, local copies, waits for them, and re-layouts: 5.51 us -> 12.2 us
    dynamic_slice x12 -> x0, local copies, waits for them, and re-layouts: 5.96 us -> none  [the longest x9 4.48 us: take(): lax.dynamic_index_in_dim(a, source, 0, False)]
  transfers between devices with their start and end apart: 3 -> 21, of which waited for: 2 -> 7; matrix products, arithmetic and copies ran while one was open for 9% -> 24% of each run, Pallas kernels for 0% -> 0%
where the time goes in v1:
time: 85.4 us; the launch traced here: 84.8 us
  starting transfers between devices  33.1 us (39%)
  local copies, waits for them, and re-layouts  23.6 us (28%)
  waiting for transfers between devices  8.04 us (9%)
  matrix products  7.85 us (9%)
  blocking collectives  5.76 us (7%)
  other arithmetic  5.63 us (7%)
    ppermute x21, starting transfers between devices, shifted(): lax.ppermute(value, axis, [(i, (i + shift) % count) for i in range(count)])  33.1 us
    unnamed x19, local copies, waits for them, and re-layouts  12.2 us
    ppermute x21, waiting for transfers between devices, shifted(): lax.ppermute(value, axis, [(i, (i + shift) % count) for i in range(count)])  8.04 us
    all_gather x1, blocking collectives, body(): lax.all_gather(updated_master.astype(jnp.bfloat16), 'roll', axis=0, tiled...  5.76 us
    reshape x2, local copies, waits for them, and re-layouts, body(): visible = jnp.repeat(visible, head_group, axis=0)  3.48 us
    dot_general x1, matrix products, body(): dprob = jnp.dot(do_rows, value_all.T, preferred_element_type=jnp.float32)  2.18 us
    dot_general x1, matrix products, body(): jnp.dot(dscore_half, key_all, preferred_element_type=jnp.float32)  2.05 us
    convert_element_type x1, other arithmetic, body(): updated_master.astype(jnp.bfloat16)  1.77 us
  transfers between devices with their start and end apart: 21, of which 7 were waited for; matrix products, arithmetic and copies ran while one was open for 24% of the time, Pallas kernels for 0%

profile of v1, /device:TPU:0, one launch (start us, length us, event | category | flops | bytes accessed | tf_op | source)
XLA Modules:
  0.0 84.8 jit_solution(12671253236670567517)
XLA Ops:
  0.7 1.6 %constant_dynamic-update-slice_fusion.1 = (bf16[128,256]{1,0:T(8,128)(2,1)}, bf16[1024,256]{1,0:T(8,128)(2,1)}) fusion(bf16[128,128]{1,0:T(8,128)(2,1)} %param.16), kind=kLoop, calls=%fused_computation.70 | loop fusion | bytes 98304
  2.2 1.4 %constant_dynamic-update-slice_fusion = (bf16[128,256]{1,0:T(8,128)(2,1)}, bf16[1024,256]{1,0:T(8,128)(2,1)}) fusion(bf16[128,256]{1,0:T(8,128)(2,1)} %get-tuple-element.39, bf16[128,128]{1,0:T(8,128)(2,1)} %param.17, bf16[1024,256]{1,0:T(8,128)(2,1)} %get-tuple-element.40), kind=kLoop, calls=%fused_computation.69 | loop fusion | bytes 98304 | tf_op jit(solution)/shard_map/concatenate | solution.py:46
  3.6 3.0 %collective-permute-start = (bf16[128,256]{1,0:T(8,128)(2,1)}, bf16[128,256]{1,0:T(8,128)(2,1)}, u32[]{:S(2)}, u32[]{:S(2)}) collective-permute-start(bf16[128,256]{1,0:T(8,128)(2,1)} %get-tuple-element.37), channel_id=1, source_target_pairs={{0,4},{4,8},{8,12},{12,16},{16,20},{20,24},{24,28},{28,0},{1,5},{5... | collective-permute-start | bytes 196616 | tf_op jit(solution)/shard_map/ppermute | solution.py:17
  6.6 1.6 %collective-permute-start.1 = (bf16[128,256]{1,0:T(8,128)(2,1)}, bf16[128,256]{1,0:T(8,128)(2,1)}, u32[]{:S(2)}, u32[]{:S(2)}) collective-permute-start(bf16[128,256]{1,0:T(8,128)(2,1)} %get-tuple-element.37), channel_id=1, source_target_pairs={{0,8},{4,12},{8,16},{12,20},{16,24},{20,28},{24,0},{28,4},{1,9},{5... | collective-permute-start | bytes 196616 | tf_op jit(solution)/shard_map/ppermute | solution.py:17
  8.2 2.5 %collective-permute-start.2 = (bf16[128,256]{1,0:T(8,128)(2,1)}, bf16[128,256]{1,0:T(8,128)(2,1)}, u32[]{:S(2)}, u32[]{:S(2)}) collective-permute-start(bf16[128,256]{1,0:T(8,128)(2,1)} %get-tuple-element.37), channel_id=1, source_target_pairs={{0,12},{4,16},{8,20},{12,24},{16,28},{20,0},{24,4},{28,8},{1,13},{... | collective-permute-start | bytes 196616 | tf_op jit(solution)/shard_map/ppermute | solution.py:17
  12.0 2.6 %collective-permute-start.4 = (bf16[128,256]{1,0:T(8,128)(2,1)}, bf16[128,256]{1,0:T(8,128)(2,1)}, u32[]{:S(2)}, u32[]{:S(2)}) collective-permute-start(bf16[128,256]{1,0:T(8,128)(2,1)} %get-tuple-element.37), channel_id=1, source_target_pairs={{0,20},{4,24},{8,28},{12,0},{16,4},{20,8},{24,12},{28,16},{1,21},{... | collective-permute-start | bytes 196616 | tf_op jit(solution)/shard_map/ppermute | solution.py:17
  20.0 2.1 %copy.21 = pred[768,1024]{0,1:T(32,128)(4,1)S(1)} copy(pred[768,1024]{1,0:T(32,128)(4,1)} %reshape.73) | data formatting | bytes 1572864 | tf_op jit(solution)/shard_map/reshape | solution.py:60
  24.8 1.5 %constant_dynamic-update-slice_fusion.8 = bf16[1024,256]{1,0:T(8,128)(2,1)} fusion(bf16[1024,256]{1,0:T(8,128)(2,1)} %get-tuple-element.38, bf16[128,256]{1,0:T(8,128)(2,1)} %collective-permute-done), kind=kLoop, calls=%fused_computation.77 | loop fusion | bytes 131072
  27.7 1.5 %constant_dynamic-update-slice_fusion.7 = bf16[1024,256]{1,0:T(8,128)(2,1)} fusion(bf16[1024,256]{1,0:T(8,128)(2,1)} %constant_dynamic-update-slice_fusion.8, bf16[128,256]{1,0:T(8,128)(2,1)} %collective-permute-done.1), kind=kLoop, calls=%fused_computation.76 | loop fusion | bytes 131072
  29.2 1.5 %constant_dynamic-update-slice_fusion.6 = bf16[1024,256]{1,0:T(8,128)(2,1)} fusion(bf16[1024,256]{1,0:T(8,128)(2,1)} %constant_dynamic-update-slice_fusion.7, bf16[128,256]{1,0:T(8,128)(2,1)} %collective-permute-done.2), kind=kLoop, calls=%fused_computation.75 | loop fusion | bytes 131072
  30.7 1.5 %constant_dynamic-update-slice_fusion.5 = bf16[1024,256]{1,0:T(8,128)(2,1)} fusion(bf16[1024,256]{1,0:T(8,128)(2,1)} %constant_dynamic-update-slice_fusion.6, bf16[128,256]{1,0:T(8,128)(2,1)} %collective-permute-done.3), kind=kLoop, calls=%fused_computation.74 | loop fusion | bytes 131072
  32.1 1.5 %constant_dynamic-update-slice_fusion.4 = bf16[1024,256]{1,0:T(8,128)(2,1)} fusion(bf16[1024,256]{1,0:T(8,128)(2,1)} %constant_dynamic-update-slice_fusion.5, bf16[128,256]{1,0:T(8,128)(2,1)} %collective-permute-done.4), kind=kLoop, calls=%fused_computation.73 | loop fusion | bytes 131072
  34.9 1.6 %fusion.3 = (f32[768]{0:T(1024)S(1)}, f32[1024,768]{1,0:T(8,128)S(1)}) fusion(pred[768,1024]{0,1:T(32,128)(4,1)S(1)} %copy.21, bf16[768,128]{1,0:T(8,128)(2,1)S(1)} %reshape.74, bf16[1024,256]{1,0:T(8,128)(2,1)} %constant_dynamic-update-slice_fusion.2), kind=kOutput, calls=%fused_computation.10 | convolution fusion | flops 203685120 | bytes 4393984 | tf_op jit(solution)/shard_map/dot_general | solution.py:61
  37.5 2.2 %fusion = (f32[768]{0:T(1024)S(1)}, f32[1024,768]{1,0:T(8,128)S(1)}) fusion(pred[768,1024]{0,1:T(32,128)(4,1)S(1)} %copy.21, f32[768]{0:T(1024)S(1)} %log_add_fusion, f32[1024,768]{1,0:T(8,128)S(1)} %get-tuple-element.44, bf16[768,128]{1,0:T(8,128)(2,1)S(1)} %reshape.75, bf16[1024,256]{1,0:T(8,128)(2,1)} %constant_dynamic-update-slice_fusion.2), kind=kOutput, calls=%fused_computation.4 | convolution fusion | flops 206044416 | bytes 7542784 | tf_op jit(solution)/shard_map/dot_general | solution.py:67
  46.9 3.5 %collective-permute-start.10 = (bf16[128,256]{0,1:T(8,128)(2,1)}, bf16[128,256]{0,1:T(8,128)(2,1)S(1)}, u32[]{:S(2)}, u32[]{:S(2)}) collective-permute-start(bf16[128,256]{0,1:T(8,128)(2,1)} %get-tuple-element.33), channel_id=1, source_target_pairs={{0,16},{4,20},{8,24},{12,28},{16,0},{20,4},{24,8},{28,12},{1,17},{... | collective-permute-start | bytes 196616 | tf_op jit(solution)/shard_map/ppermute | solution.py:17
  50.3 1.8 %collective-permute-done.13 = bf16[128,256]{0,1:T(8,128)(2,1)S(1)} collective-permute-done((bf16[128,256]{0,1:T(8,128)(2,1)S(1)}, bf16[128,256]{0,1:T(8,128)(2,1)S(1)}, u32[]{:S(2)}, u32[]{:S(2)}) %collective-permute-start.13) | collective-permute-done | bytes 65568 | tf_op jit(solution)/shard_map/ppermute | solution.py:17
  52.7 1.5 %collective-permute-start.7 = (bf16[128,256]{0,1:T(8,128)(2,1)S(1)}, bf16[128,256]{0,1:T(8,128)(2,1)S(1)}, u32[]{:S(2)}, u32[]{:S(2)}) collective-permute-start(bf16[128,256]{0,1:T(8,128)(2,1)S(1)} %get-tuple-element.30), channel_id=1, source_target_pairs={{0,28},{4,0},{8,4},{12,8},{16,12},{20,16},{24,20},{28,24},{1,29},{... | collective-permute-start | bytes 196616 | tf_op jit(solution)/shard_map/ppermute | solution.py:17
  58.1 4.5 %collective-permute-start.20 = (bf16[256,128]{1,0:T(8,128)(2,1)S(1)}, bf16[256,128]{1,0:T(8,128)(2,1)S(1)}, u32[]{:S(2)}, u32[]{:S(2)}) collective-permute-start(bf16[256,128]{1,0:T(8,128)(2,1)S(1)} %get-tuple-element.24), channel_id=1, source_target_pairs={{0,28},{4,0},{8,4},{12,8},{16,12},{20,16},{24,20},{28,24},{1,29},{... | collective-permute-start | bytes 196616 | tf_op jit(solution)/shard_map/ppermute | solution.py:17
  63.4 2.2 %collective-permute-start.17 = (bf16[256,128]{1,0:T(8,128)(2,1)}, bf16[256,128]{1,0:T(8,128)(2,1)S(1)}, u32[]{:S(2)}, u32[]{:S(2)}) collective-permute-start(bf16[256,128]{1,0:T(8,128)(2,1)} %get-tuple-element.27), channel_id=1, source_target_pairs={{0,16},{4,20},{8,24},{12,28},{16,0},{20,4},{24,8},{28,12},{1,17},{... | collective-permute-start | bytes 196616 | tf_op jit(solution)/shard_map/ppermute | solution.py:17
  66.5 2.7 %collective-permute-start.15 = (bf16[256,128]{1,0:T(8,128)(2,1)}, bf16[256,128]{1,0:T(8,128)(2,1)S(1)}, u32[]{:S(2)}, u32[]{:S(2)}) collective-permute-start(bf16[256,128]{1,0:T(8,128)(2,1)} %get-tuple-element.29), channel_id=1, source_target_pairs={{0,8},{4,12},{8,16},{12,20},{16,24},{20,28},{24,0},{28,4},{1,9},{5... | collective-permute-start | bytes 196616 | tf_op jit(solution)/shard_map/ppermute | solution.py:17
  69.3 2.0 %fusion.10 = bf16[768,128]{1,0:T(8,128)(2,1)S(1)} fusion(bf16[768,1024]{0,1:T(8,128)(2,1)} %copy-done.1, bf16[1024,256]{1,0:T(8,128)(2,1)} %constant_dynamic-update-slice_fusion.2), kind=kOutput, calls=%fused_computation.18 | convolution fusion | flops 201523200 | bytes 2031616 | tf_op jit(solution)/shard_map/dot_general | solution.py:72
  73.0 2.1 %collective-permute-done.16 = bf16[256,128]{1,0:T(8,128)(2,1)S(1)} collective-permute-done((bf16[256,128]{1,0:T(8,128)(2,1)}, bf16[256,128]{1,0:T(8,128)(2,1)S(1)}, u32[]{:S(2)}, u32[]{:S(2)}) %collective-permute-start.16) | collective-permute-done | bytes 65568 | tf_op jit(solution)/shard_map/ppermute | solution.py:17
  76.5 1.8 %fusion.39 = (bf16[256,128]{1,0:T(8,128)(2,1)S(1)}, f32[256,128]{1,0:T(8,128)}, f32[256,128]{1,0:T(8,128)}, f32[256,128]{1,0:T(8,128)}) fusion(f32[256,128]{1,0:T(8,128)S(1)} %copy-done.3, f32[256,128]{1,0:T(8,128)S(1)} %copy-done.4, f32[256,128]{1,0:T(8,128)} %param.21, bf16[256,128]{1,0:T(8,128)(2,1)S(1)} %collective-permute-done.20, ...), kind=kLoop, calls=%fused_computation.100 | loop fusion | flops 1015808 | bytes 1376260 | tf_op jit(solution)/shard_map/convert_element_type | solution.py:111
  78.3 5.8 %all_gather.3 = bf16[1024,128]{1,0:T(8,128)(2,1)S(1)} all-gather(bf16[256,128]{1,0:T(8,128)(2,1)S(1)} %get-tuple-element.19), channel_id=1, replica_groups=mesh['ctx'=8,'roll'=4] {'roll'}, dimensions={0}, use_global_device_ids=true | all-gather | bytes 327680 | tf_op jit(solution)/shard_map/all_gather | solution.py:111
  (69 shorter events, 29.9 us)
Async XLA Ops:
  0.6 56.4 %copy-start = (bf16[8192,128]{1,0:T(8,128)(2,1)S(1)}, bf16[8192,128]{1,0:T(8,128)(2,1)}, u32[]{:S(2)}) copy-start(bf16[8192,128]{1,0:T(8,128)(2,1)} %param.14) | copy-start | bytes 6291460
  3.6 19.8 %collective-permute-start = (bf16[128,256]{1,0:T(8,128)(2,1)}, bf16[128,256]{1,0:T(8,128)(2,1)}, u32[]{:S(2)}, u32[]{:S(2)}) collective-permute-start(bf16[128,256]{1,0:T(8,128)(2,1)} %get-tuple-element.37), channel_id=1, source_target_pairs={{0,4},{4,8},{8,12},{12,16},{16,20},{20,24},{24,28},{28,0},{1,5},{5... | collective-permute-start | bytes 196616 | tf_op jit(solution)/shard_map/ppermute | solution.py:17
  6.6 19.7 %collective-permute-start.1 = (bf16[128,256]{1,0:T(8,128)(2,1)}, bf16[128,256]{1,0:T(8,128)(2,1)}, u32[]{:S(2)}, u32[]{:S(2)}) collective-permute-start(bf16[128,256]{1,0:T(8,128)(2,1)} %get-tuple-element.37), channel_id=1, source_target_pairs={{0,8},{4,12},{8,16},{12,20},{16,24},{20,28},{24,0},{28,4},{1,9},{5... | collective-permute-start | bytes 196616 | tf_op jit(solution)/shard_map/ppermute | solution.py:17
  8.2 21.0 %collective-permute-start.2 = (bf16[128,256]{1,0:T(8,128)(2,1)}, bf16[128,256]{1,0:T(8,128)(2,1)}, u32[]{:S(2)}, u32[]{:S(2)}) collective-permute-start(bf16[128,256]{1,0:T(8,128)(2,1)} %get-tuple-element.37), channel_id=1, source_target_pairs={{0,12},{4,16},{8,20},{12,24},{16,28},{20,0},{24,4},{28,8},{1,13},{... | collective-permute-start | bytes 196616 | tf_op jit(solution)/shard_map/ppermute | solution.py:17
  10.7 19.9 %collective-permute-start.3 = (bf16[128,256]{1,0:T(8,128)(2,1)}, bf16[128,256]{1,0:T(8,128)(2,1)}, u32[]{:S(2)}, u32[]{:S(2)}) collective-permute-start(bf16[128,256]{1,0:T(8,128)(2,1)} %get-tuple-element.37), channel_id=1, source_target_pairs={{0,16},{4,20},{8,24},{12,28},{16,0},{20,4},{24,8},{28,12},{1,17},{... | collective-permute-start | bytes 196616 | tf_op jit(solution)/shard_map/ppermute | solution.py:17
  12.0 20.2 %collective-permute-start.4 = (bf16[128,256]{1,0:T(8,128)(2,1)}, bf16[128,256]{1,0:T(8,128)(2,1)}, u32[]{:S(2)}, u32[]{:S(2)}) collective-permute-start(bf16[128,256]{1,0:T(8,128)(2,1)} %get-tuple-element.37), channel_id=1, source_target_pairs={{0,20},{4,24},{8,28},{12,0},{16,4},{20,8},{24,12},{28,16},{1,21},{... | collective-permute-start | bytes 196616 | tf_op jit(solution)/shard_map/ppermute | solution.py:17
  23.4 10.2 %collective-permute-start.5 = (bf16[128,256]{1,0:T(8,128)(2,1)}, bf16[128,256]{1,0:T(8,128)(2,1)S(1)}, u32[]{:S(2)}, u32[]{:S(2)}) collective-permute-start(bf16[128,256]{1,0:T(8,128)(2,1)} %get-tuple-element.37), channel_id=1, source_target_pairs={{0,24},{4,28},{8,0},{12,4},{16,8},{20,12},{24,16},{28,20},{1,25},{... | collective-permute-start | bytes 196616 | tf_op jit(solution)/shard_map/ppermute | solution.py:17
  26.3 7.9 %collective-permute-start.6 = (bf16[128,256]{1,0:T(8,128)(2,1)}, bf16[128,256]{1,0:T(8,128)(2,1)S(1)}, u32[]{:S(2)}, u32[]{:S(2)}) collective-permute-start(bf16[128,256]{1,0:T(8,128)(2,1)} %get-tuple-element.37), channel_id=1, source_target_pairs={{0,28},{4,0},{8,4},{12,8},{16,12},{20,16},{24,20},{28,24},{1,29},{... | collective-permute-start | bytes 196616 | tf_op jit(solution)/shard_map/ppermute | solution.py:17
  44.4 32.1 %copy-start.3 = (f32[256,128]{1,0:T(8,128)S(1)}, f32[256,128]{1,0:T(8,128)}, u32[]{:S(2)}) copy-start(f32[256,128]{1,0:T(8,128)} %param.19) | copy-start | bytes 393220
  44.4 32.1 %copy-start.4 = (f32[256,128]{1,0:T(8,128)S(1)}, f32[256,128]{1,0:T(8,128)}, u32[]{:S(2)}) copy-start(f32[256,128]{1,0:T(8,128)} %param.20) | copy-start | bytes 393220
  44.4 7.7 %collective-permute-start.13 = (bf16[128,256]{0,1:T(8,128)(2,1)S(1)}, bf16[128,256]{0,1:T(8,128)(2,1)S(1)}, u32[]{:S(2)}, u32[]{:S(2)}) collective-permute-start(bf16[128,256]{0,1:T(8,128)(2,1)S(1)} %get-tuple-element.35), channel_id=1, source_target_pairs={{0,4},{4,8},{8,12},{12,16},{16,20},{20,24},{24,28},{28,0},{1,5},{5... | collective-permute-start | bytes 196616 | tf_op jit(solution)/shard_map/ppermute | solution.py:17
  45.0 7.7 %collective-permute-start.12 = (bf16[128,256]{0,1:T(8,128)(2,1)S(1)}, bf16[128,256]{0,1:T(8,128)(2,1)S(1)}, u32[]{:S(2)}, u32[]{:S(2)}) collective-permute-start(bf16[128,256]{0,1:T(8,128)(2,1)S(1)} %get-tuple-element.36), channel_id=1, source_target_pairs={{0,8},{4,12},{8,16},{12,20},{16,24},{20,28},{24,0},{28,4},{1,9},{5... | collective-permute-start | bytes 196616 | tf_op jit(solution)/shard_map/ppermute | solution.py:17
  45.7 9.8 %collective-permute-start.11 = (bf16[128,256]{0,1:T(8,128)(2,1)}, bf16[128,256]{0,1:T(8,128)(2,1)S(1)}, u32[]{:S(2)}, u32[]{:S(2)}) collective-permute-start(bf16[128,256]{0,1:T(8,128)(2,1)} %get-tuple-element.34), channel_id=1, source_target_pairs={{0,12},{4,16},{8,20},{12,24},{16,28},{20,0},{24,4},{28,8},{1,13},{... | collective-permute-start | bytes 196616 | tf_op jit(solution)/shard_map/ppermute | solution.py:17
  46.9 8.6 %collective-permute-start.10 = (bf16[128,256]{0,1:T(8,128)(2,1)}, bf16[128,256]{0,1:T(8,128)(2,1)S(1)}, u32[]{:S(2)}, u32[]{:S(2)}) collective-permute-start(bf16[128,256]{0,1:T(8,128)(2,1)} %get-tuple-element.33), channel_id=1, source_target_pairs={{0,16},{4,20},{8,24},{12,28},{16,0},{20,4},{24,8},{28,12},{1,17},{... | collective-permute-start | bytes 196616 | tf_op jit(solution)/shard_map/ppermute | solution.py:17
  50.3 5.2 %collective-permute-start.9 = (bf16[128,256]{0,1:T(8,128)(2,1)S(1)}, bf16[128,256]{0,1:T(8,128)(2,1)S(1)}, u32[]{:S(2)}, u32[]{:S(2)}) collective-permute-start(bf16[128,256]{0,1:T(8,128)(2,1)S(1)} %get-tuple-element.32), channel_id=1, source_target_pairs={{0,20},{4,24},{8,28},{12,0},{16,4},{20,8},{24,12},{28,16},{1,21},{... | collective-permute-start | bytes 196616 | tf_op jit(solution)/shard_map/ppermute | solution.py:17
  52.1 4.5 %collective-permute-start.8 = (bf16[128,256]{0,1:T(8,128)(2,1)S(1)}, bf16[128,256]{0,1:T(8,128)(2,1)S(1)}, u32[]{:S(2)}, u32[]{:S(2)}) collective-permute-start(bf16[128,256]{0,1:T(8,128)(2,1)S(1)} %get-tuple-element.31), channel_id=1, source_target_pairs={{0,24},{4,28},{8,0},{12,4},{16,8},{20,12},{24,16},{28,20},{1,25},{... | collective-permute-start | bytes 196616 | tf_op jit(solution)/shard_map/ppermute | solution.py:17
  52.7 4.3 %collective-permute-start.7 = (bf16[128,256]{0,1:T(8,128)(2,1)S(1)}, bf16[128,256]{0,1:T(8,128)(2,1)S(1)}, u32[]{:S(2)}, u32[]{:S(2)}) collective-permute-start(bf16[128,256]{0,1:T(8,128)(2,1)S(1)} %get-tuple-element.30), channel_id=1, source_target_pairs={{0,28},{4,0},{8,4},{12,8},{16,12},{20,16},{24,20},{28,24},{1,29},{... | collective-permute-start | bytes 196616 | tf_op jit(solution)/shard_map/ppermute | solution.py:17
  58.1 8.4 %collective-permute-start.20 = (bf16[256,128]{1,0:T(8,128)(2,1)S(1)}, bf16[256,128]{1,0:T(8,128)(2,1)S(1)}, u32[]{:S(2)}, u32[]{:S(2)}) collective-permute-start(bf16[256,128]{1,0:T(8,128)(2,1)S(1)} %get-tuple-element.24), channel_id=1, source_target_pairs={{0,28},{4,0},{8,4},{12,8},{16,12},{20,16},{24,20},{28,24},{1,29},{... | collective-permute-start | bytes 196616 | tf_op jit(solution)/shard_map/ppermute | solution.py:17
  62.7 6.6 %collective-permute-start.19 = (bf16[256,128]{1,0:T(8,128)(2,1)S(1)}, bf16[256,128]{1,0:T(8,128)(2,1)S(1)}, u32[]{:S(2)}, u32[]{:S(2)}) collective-permute-start(bf16[256,128]{1,0:T(8,128)(2,1)S(1)} %get-tuple-element.25), channel_id=1, source_target_pairs={{0,24},{4,28},{8,0},{12,4},{16,8},{20,12},{24,16},{28,20},{1,25},{... | collective-permute-start | bytes 196616 | tf_op jit(solution)/shard_map/ppermute | solution.py:17
  62.7 10.3 %collective-permute-start.18 = (bf16[256,128]{1,0:T(8,128)(2,1)}, bf16[256,128]{1,0:T(8,128)(2,1)S(1)}, u32[]{:S(2)}, u32[]{:S(2)}) collective-permute-start(bf16[256,128]{1,0:T(8,128)(2,1)} %get-tuple-element.26), channel_id=1, source_target_pairs={{0,20},{4,24},{8,28},{12,0},{16,4},{20,8},{24,12},{28,16},{1,21},{... | collective-permute-start | bytes 196616 | tf_op jit(solution)/shard_map/ppermute | solution.py:17
  63.4 9.6 %collective-permute-start.17 = (bf16[256,128]{1,0:T(8,128)(2,1)}, bf16[256,128]{1,0:T(8,128)(2,1)S(1)}, u32[]{:S(2)}, u32[]{:S(2)}) collective-permute-start(bf16[256,128]{1,0:T(8,128)(2,1)} %get-tuple-element.27), channel_id=1, source_target_pairs={{0,16},{4,20},{8,24},{12,28},{16,0},{20,4},{24,8},{28,12},{1,17},{... | collective-permute-start | bytes 196616 | tf_op jit(solution)/shard_map/ppermute | solution.py:17
  65.6 9.6 %collective-permute-start.16 = (bf16[256,128]{1,0:T(8,128)(2,1)}, bf16[256,128]{1,0:T(8,128)(2,1)S(1)}, u32[]{:S(2)}, u32[]{:S(2)}) collective-permute-start(bf16[256,128]{1,0:T(8,128)(2,1)} %get-tuple-element.28), channel_id=1, source_target_pairs={{0,12},{4,16},{8,20},{12,24},{16,28},{20,0},{24,4},{28,8},{1,13},{... | collective-permute-start | bytes 196616 | tf_op jit(solution)/shard_map/ppermute | solution.py:17
  66.5 8.7 %collective-permute-start.15 = (bf16[256,128]{1,0:T(8,128)(2,1)}, bf16[256,128]{1,0:T(8,128)(2,1)S(1)}, u32[]{:S(2)}, u32[]{:S(2)}) collective-permute-start(bf16[256,128]{1,0:T(8,128)(2,1)} %get-tuple-element.29), channel_id=1, source_target_pairs={{0,8},{4,12},{8,16},{12,20},{16,24},{20,28},{24,0},{28,4},{1,9},{5... | collective-permute-start | bytes 196616 | tf_op jit(solution)/shard_map/ppermute | solution.py:17
  69.2 7.3 %collective-permute-start.14 = (bf16[256,128]{1,0:T(8,128)(2,1)}, bf16[256,128]{1,0:T(8,128)(2,1)}, u32[]{:S(2)}, u32[]{:S(2)}) collective-permute-start(bf16[256,128]{1,0:T(8,128)(2,1)} %get-tuple-element.23), channel_id=1, source_target_pairs={{0,4},{4,8},{8,12},{12,16},{16,20},{20,24},{24,28},{28,0},{1,5},{5... | collective-permute-start | bytes 196616 | tf_op jit(solution)/shard_map/ppermute | solution.py:17
  (2 other events, 22.6 us)
